TPU v7x, 256 devices: a whole 4x4x8 slice. The times are simulated.
256 devices in a mesh: row: 16 (over x_lo, z), col: 16 (over x_hi, y, core).
Axes of the slice: x: 4 (x_hi: 2, x_lo: 2; x = x_hi * 2 + x_lo), y: 4, z: 8, core: 2. Of those that a mesh axis runs over, the one named last changes fastest.
Arguments:
- sp2_branch: int32 [3], replicated, may hold values from 0 to 1, as said below
- p0_occupancy: int32 [32, 32], replicated, may hold values from 0 to 1, as said below
- p1_occupancy: int32 [32, 32], replicated, may hold values from 0 to 1, as said below
- p0_columns: bfloat16 [73728, 512], P('col'), as said below
- p1_tiles: bfloat16 [3, 8192, 8192], P(None, 'row', 'col'), may hold values from -6 to 6, as said below
Outputs:
- p1_next: bfloat16 [3, 8192, 8192], P(None, 'row', 'col')
Inputs may be any that keep to these rules, and one draw needn't show every extreme that they name: `sp2_branch`: both values occur among the displacements. `p0_occupancy`: symmetric; every diagonal block is 1; blocks more than 8 apart around the circle of 32 blocks are 0. `p1_occupancy`: symmetric. `p0_columns`: the strips describe one symmetric matrix: a stored entry at row u and column v equals the stored entry at row v and column u; blocks more than 8 apart around the circle are zero. `p1_tiles`: each displacement's matrix is symmetric.
All inputs are finite; a program needn't handle non-finite values.
Results may differ from a plain program's by a relative error of at most 0.001.
Values may be sent and summed in bfloat16 or wider, within the bound.
No kernel may reach another device: no remote copies, remote signals or barrier semaphores. Data moves between devices by JAX's collectives and lax.ppermute only.
A program may use at most 192 MiB of HBM per device.

v0:
```python
import jax
import jax.numpy as jnp
from jax import lax
from jax.sharding import PartitionSpec as P

BLK = 256


def from_behind(array, axis, by):
    length = lax.axis_size(axis)
    return lax.ppermute(array, axis, [(i, (i + by) % length) for i in range(length)])


def broadcast(array, axis, root):
    mine = lax.axis_index(axis) == root
    return lax.psum(jnp.where(mine, array, jnp.zeros_like(array)), axis)


def mask_blocks(values, occupancy):
    leading = values.shape[:-2]
    row_blocks = values.shape[-2] // BLK
    col_blocks = values.shape[-1] // BLK
    shaped = values.reshape(leading + (row_blocks, BLK, col_blocks, BLK))
    weight = occupancy.astype(values.dtype)[:, None, :, None]
    return (shaped * weight).reshape(values.shape)


def right_product(left_op, right_op):
    return jnp.einsum("drc,ck->drk", left_op, right_op, preferred_element_type=jnp.float32)


def left_product(left_op, right_op):
    return jnp.einsum("kr,dkc->drc", left_op, right_op, preferred_element_type=jnp.float32)


def column_term(summed, incoming, factor):
    return summed + right_product(incoming, factor)


def row_term(summed, incoming, factor):
    return summed + left_product(factor, incoming)


def col_move(values, distance):
    return from_behind(values, "col", distance)


def row_move(values, distance):
    return from_behind(values, "row", distance)


def body(sp2_branch, p0_occupancy, p1_occupancy, p0_columns, p1_tiles):
    col_count = lax.axis_size("col")
    col_width = p0_columns.shape[1]
    row_height = p1_tiles.shape[1]
    col_blocks = col_width // BLK
    row_blocks = row_height // BLK
    strip_blocks = p0_columns.shape[0] // BLK
    band_half = (strip_blocks - col_blocks) // 2
    all_blocks = col_blocks * col_count
    col_span = band_half // col_blocks
    row_span = band_half // row_blocks
    row_at = lax.axis_index("row")
    col_at = lax.axis_index("col")
    own_occ = lax.dynamic_slice(
        p1_occupancy, (row_at * row_blocks, col_at * col_blocks), (row_blocks, col_blocks)
    )
    p1_local = mask_blocks(p1_tiles, own_occ)
    tripled = jnp.concatenate([p0_occupancy, p0_occupancy, p0_occupancy], axis=0)
    strip_occ = lax.dynamic_slice(
        tripled,
        (col_at * col_blocks - band_half + all_blocks, col_at * col_blocks),
        (strip_blocks, col_blocks),
    )
    strip_local = mask_blocks(p0_columns, strip_occ)

    def col_add(summed, incoming, distance):
        factor = strip_local[
            (distance + col_span) * col_width : (distance + col_span + 1) * col_width, :
        ]
        return column_term(summed, incoming, factor)

    summed_col = jnp.zeros(p1_local.shape, jnp.float32)
    summed_col = col_add(summed_col, p1_local, 0)
    moving = p1_local
    for distance in range(1, col_span + 1):
        moving = col_move(moving, 1)
        summed_col = col_add(summed_col, moving, -distance)
    moving = from_behind(moving, "col", -2 * col_span)
    summed_col = col_add(summed_col, moving, col_span)
    for distance in range(col_span - 1, 0, -1):
        moving = col_move(moving, 1)
        summed_col = col_add(summed_col, moving, distance)
    owner_col = row_at * row_blocks // col_blocks
    shared = broadcast(strip_local, "col", owner_col)

    def row_add(summed, incoming, distance):
        factor = shared[
            (distance + row_span) * row_height : (distance + row_span + 1) * row_height, :
        ]
        return row_term(summed, incoming, factor)

    summed_row = jnp.zeros(p1_local.shape, jnp.float32)
    summed_row = row_add(summed_row, p1_local, 0)
    moving = p1_local
    for distance in range(1, row_span + 1):
        moving = row_move(moving, 1)
        summed_row = row_add(summed_row, moving, -distance)
    moving = from_behind(moving, "row", -2 * row_span)
    summed_row = row_add(summed_row, moving, row_span)
    for distance in range(row_span - 1, 0, -1):
        moving = row_move(moving, 1)
        summed_row = row_add(summed_row, moving, distance)
    bracket = summed_col + summed_row
    squared = (sp2_branch == 1)[:, None, None]
    chosen = jnp.where(squared, bracket, 2.0 * p1_local.astype(jnp.float32) - bracket)
    return mask_blocks(chosen, own_occ).astype(jnp.bfloat16)


def solution(mesh):
    in_specs = (P(), P(), P(), P("col", None), P(None, "row", "col"))
    out_specs = P(None, "row", "col")
    return jax.shard_map(body, mesh=mesh, in_specs=in_specs, out_specs=out_specs, check_vma=False)
```

profile of v0, /device:TPU:2, one launch (start us, length us, event | category | flops | bytes accessed | tf_op | source)
XLA Modules:
  0.0 573.2 jit_solution(15829006812120409035)
XLA Ops:
  6.5 0.8 dynamic-slice_convert_fusion
  7.3 0.3 mul.56
  7.7 0.1 copy.64
  7.8 1.6 broadcast_multiply_fusion.1
  9.4 2.0 collective-permute-start.8
  11.4 38.3 %collective-permute-done.8 = bf16[3,512,512]{2,1,0:T(8,128)(2,1)S(1)} collective-permute-done((bf16[3,512,512]{2,1,0:T(8,128)(2,1)S(1)}, bf16[3,512,512]{2,1,0:T(8,128)(2,1)S(1)}, u32[]{:S(2)}, u32[]{:S(2)}) %collective-permute-start.8) | collective-permute-done | bytes 1572896 | tf_op jit(solution)/shard_map/ppermute | solution.py:11
  49.7 52.7 %collective-permute-done = bf16[3,512,512]{2,1,0:T(8,128)(2,1)} collective-permute-done((bf16[3,512,512]{2,1,0:T(8,128)(2,1)S(1)}, bf16[3,512,512]{2,1,0:T(8,128)(2,1)}, u32[]{:S(2)}, u32[]{:S(2)}) %collective-permute-start) | collective-permute-done | bytes 1572896 | tf_op jit(solution)/shard_map/ppermute | solution.py:11
  102.3 0.0 collective-permute-start.1
  102.3 0.1 copy.24
  102.4 0.1 fusion.12
  102.5 0.1 copy.27
  102.6 2.5 mul.60
  105.1 0.0 slice-start
  105.1 0.0 slice-start.1
  105.2 1.0 copy.65
  106.1 0.1 collective-permute-start.10
  106.2 53.6 %collective-permute-done.1 = bf16[3,512,512]{2,1,0:T(8,128)(2,1)} collective-permute-done((bf16[3,512,512]{2,1,0:T(8,128)(2,1)}, bf16[3,512,512]{2,1,0:T(8,128)(2,1)}, u32[]{:S(2)}, u32[]{:S(2)}) %collective-permute-start.1) | collective-permute-done | bytes 1572896 | tf_op jit(solution)/shard_map/ppermute | solution.py:11
  159.8 2.7 multiply_select_fusion
  162.5 0.0 all-reduce.2.cloned.1.call-update
  162.5 0.1 collective-permute-start.11
  162.6 63.5 %collective-permute-done.2 = bf16[3,512,512]{2,1,0:T(8,128)(2,1)S(1)} collective-permute-done((bf16[3,512,512]{2,1,0:T(8,128)(2,1)}, bf16[3,512,512]{2,1,0:T(8,128)(2,1)S(1)}, u32[]{:S(2)}, u32[]{:S(2)}) %collective-permute-start.2) | collective-permute-done | bytes 1572896 | tf_op jit(solution)/shard_map/ppermute | solution.py:11
  226.1 0.0 collective-permute-start.3
  226.1 8.0 %reshape.24 = bf16[18,256,2,256]{3,2,1,0:T(2,128)(2,1)} reshape(bf16[4608,512]{1,0:T(8,128)(2,1)} %param.8) | data formatting | bytes 9437184 | tf_op jit(solution)/shard_map/reshape | solution.py:23
  234.1 0.5 collective-permute-start.12
  234.6 41.9 %collective-permute-done.3 = bf16[3,512,512]{2,1,0:T(8,128)(2,1)} collective-permute-done((bf16[3,512,512]{2,1,0:T(8,128)(2,1)S(1)}, bf16[3,512,512]{2,1,0:T(8,128)(2,1)}, u32[]{:S(2)}, u32[]{:S(2)}) %collective-permute-start.3) | collective-permute-done | bytes 1572896 | tf_op jit(solution)/shard_map/ppermute | solution.py:11
  276.5 2.7 collective-permute-start.4
  279.1 8.6 %broadcast_multiply_fusion = bf16[18,256,2,256]{3,2,1,0:T(2,128)(2,1)} fusion(bf16[18,256,2,256]{3,2,1,0:T(2,128)(2,1)} %reshape.24, bf16[18,2]{1,0:T(8,128)(2,1)S(1)} %copy.27), kind=kLoop, calls=%fused_computation.5 | loop fusion | flops 2359296 | bytes 9437256 | tf_op jit(solution)/shard_map/mul | solution.py:25
  287.8 0.3 mul.66
  288.1 0.1 copy.66
  288.2 6.1 %fusion.13 = (bf16[2,256,2,256]{3,2,1,0:T(2,128)(2,1)S(1)}, bf16[2,256,2,256]{3,2,1,0:T(2,128)(2,1)}, bf16[2,256,2,256]{3,2,1,0:T(2,128)(2,1)}, bf16[2,256,2,256...) fusion(bf16[18,256,2,256]{3,2,1,0:T(2,128)(2,1)} %broadcast_mul, ...), kind=kLoop, calls=%fused_computation.33 | loop fusion | bytes 9437184 | tf_op jit(solution)/shard_map/slice | solution.py:78
  294.3 1.1 reshape.26
  295.4 1.4 reshape.33
  296.8 2.2 reshape.32
  299.0 2.2 reshape.31
  301.2 2.2 reshape.30
  303.3 2.2 reshape.29
  305.5 2.2 reshape.28
  307.7 2.2 reshape.27
  309.9 2.2 reshape.25
  312.1 3.8 fusion.14
  315.8 7.7 %collective-permute-done.4 = bf16[3,512,512]{2,1,0:T(8,128)(2,1)} collective-permute-done((bf16[3,512,512]{2,1,0:T(8,128)(2,1)}, bf16[3,512,512]{2,1,0:T(8,128)(2,1)}, u32[]{:S(2)}, u32[]{:S(2)}) %collective-permute-start.4) | collective-permute-done | bytes 1572896 | tf_op jit(solution)/shard_map/ppermute | solution.py:11
  323.5 0.0 collective-permute-start.5
  323.5 4.0 fusion.15
  327.5 0.2 collective-permute-start.13
  327.7 4.0 fusion.16
  331.8 82.2 %all-reduce.2.cloned.1.call-done = bf16[4608,512]{1,0:T(8,128)(2,1)} async-done(((bf16[4608,512]{1,0:T(8,128)(2,1)}), bf16[4608,512]{1,0:T(8,128)(2,1)}) %all-reduce.2.cloned.1.call-update) | async-done | bytes 4718608 | tf_op jit(solution)/shard_map/psum | solution.py:16
  414.0 4.3 fusion.6
  418.3 4.3 fusion.7
  422.6 2.7 fusion.8
  425.3 2.7 fusion.9
  428.0 2.6 fusion.17
  430.7 4.2 fusion.5
  434.8 4.1 fusion.18
  438.9 4.1 fusion.4
  443.0 39.6 %collective-permute-done.6 = bf16[3,512,512]{2,1,0:T(8,128)(2,1)S(1)} collective-permute-done((bf16[3,512,512]{2,1,0:T(8,128)(2,1)}, bf16[3,512,512]{2,1,0:T(8,128)(2,1)S(1)}, u32[]{:S(2)}, u32[]{:S(2)}) %collective-permute-start.6) | collective-permute-done | bytes 1572896 | tf_op jit(solution)/shard_map/ppermute | solution.py:11
  482.6 4.0 fusion.19
  486.7 0.2 collective-permute-start.15
  486.9 4.2 fusion.3
  491.1 4.1 fusion.20
  495.2 2.7 fusion.2
  497.9 2.6 fusion.21
  500.5 39.3 %collective-permute-done.7 = bf16[3,512,512]{2,1,0:T(8,128)(2,1)S(1)} collective-permute-done((bf16[3,512,512]{2,1,0:T(8,128)(2,1)S(1)}, bf16[3,512,512]{2,1,0:T(8,128)(2,1)S(1)}, u32[]{:S(2)}, u32[]{:S(2)}) %collective-permute-start.7) | collective-permute-done | bytes 1572896 | tf_op jit(solution)/shard_map/ppermute | solution.py:11
  539.8 2.6 fusion.22
  542.4 23.7 %fusion.1 = bf16[3,512,512]{2,1,0:T(8,128)(2,1)} fusion(f32[3,512,512]{1,2,0:T(8,128)} %fusion.2, f32[3,512,512]{1,2,0:T(8,128)} %fusion.3, f32[3,512,512]{1,2,0:T(8,128)} %fusion.4, bf16[3,512,512]{2,1,0:T(8,128)(2,1)S(1)} %broadcast_multiply_fusion.1, f32[3,512,512]{1,2,0:T(8,128)} %fusion.5, f32[3,512,512]{1,2,0:T(8,128)} %fusion.6, ...), kind=kOutput, calls=%fused_computation.3 | convolution fusion | flops 823394304 | bytes 59768836 | tf_op jit(solution)/shard_map/kr,dkc->drc/dot_general | solution.py:33
  (47 shorter events, 0.1 us)
Async XLA Ops:
  6.5 95.8 %copy-start.12 = (s32[32,32]{1,0:T(8,128)S(1)}, s32[32,32]{1,0:T(8,128)}, u32[]{:S(2)}) copy-start(s32[32,32]{1,0:T(8,128)} %param.6) | copy-start | bytes 12292
  6.5 407.4 %all-reduce.2.cloned.1.call-start = ((), (), s32[]{:S(2)}) async-start(), calls=%async_computation | async-start | bytes 9437184 | tf_op jit(solution)/shard_map/psum | solution.py:16
  9.4 40.3 %collective-permute-start.8 = (bf16[3,512,512]{2,1,0:T(8,128)(2,1)S(1)}, bf16[3,512,512]{2,1,0:T(8,128)(2,1)S(1)}, u32[]{:S(2)}, u32[]{:S(2)}) collective-permute-start(bf16[3,512,512]{2,1,0:T(8,128)(2,1)S(1)} %broadcast_multiply_fusion.1), channel_id=1, source_target_pairs={{0,16},{16,32},{32,48},{48,64},{64,80},{80,96},{96,112},{112,128},... | collective-permute-start | bytes 4718600 | tf_op jit(solution)/shard_map/ppermute | solution.py:11
  11.4 91.0 %collective-permute-start = (bf16[3,512,512]{2,1,0:T(8,128)(2,1)S(1)}, bf16[3,512,512]{2,1,0:T(8,128)(2,1)}, u32[]{:S(2)}, u32[]{:S(2)}) collective-permute-start(bf16[3,512,512]{2,1,0:T(8,128)(2,1)S(1)} %broadcast_multiply_fusion.1), channel_id=1, source_target_pairs={{0,1},{1,2},{2,3},{3,4},{4,5},{5,6},{6,7},{7,8},{8,9},{9,10},{10,1... | collective-permute-start | bytes 4718600 | tf_op jit(solution)/shard_map/ppermute | solution.py:11
  49.7 56.5 %copy-start.8 = (bf16[3,512,512]{2,1,0:T(8,128)(2,1)}, bf16[3,512,512]{2,1,0:T(8,128)(2,1)S(1)}, u32[]{:S(2)}) copy-start(bf16[3,512,512]{2,1,0:T(8,128)(2,1)S(1)} %collective-permute-done.8) | copy-start | bytes 4718596
  49.7 56.5 %collective-permute-start.9 = (bf16[3,512,512]{2,1,0:T(8,128)(2,1)S(1)}, bf16[3,512,512]{2,1,0:T(8,128)(2,1)}, u32[]{:S(2)}, u32[]{:S(2)}) collective-permute-start(bf16[3,512,512]{2,1,0:T(8,128)(2,1)S(1)} %collective-permute-done.8), channel_id=1, source_target_pairs={{0,16},{16,32},{32,48},{48,64},{64,80},{80,96},{96,112},{112,128},... | collective-permute-start | bytes 4718600 | tf_op jit(solution)/shard_map/ppermute | solution.py:11
  102.3 57.5 %collective-permute-start.1 = (bf16[3,512,512]{2,1,0:T(8,128)(2,1)}, bf16[3,512,512]{2,1,0:T(8,128)(2,1)}, u32[]{:S(2)}, u32[]{:S(2)}) collective-permute-start(bf16[3,512,512]{2,1,0:T(8,128)(2,1)} %collective-permute-done), channel_id=1, source_target_pairs={{0,1},{1,2},{2,3},{3,4},{4,5},{5,6},{6,7},{7,8},{8,9},{9,10},{10,1... | collective-permute-start | bytes 4718600 | tf_op jit(solution)/shard_map/ppermute | solution.py:11
  105.1 54.7 %slice-start = ((s8[4718592]{0:T(1024)(128)(4,1)}), s8[4194304]{0:T(1024)(128)(4,1)S(1)}, s32[]{:S(2)}) async-start(s8[4718592]{0:T(1024)(128)(4,1)} %bitcast.68), calls=%async_computation.1 | async-start | bytes 8388608
  105.1 54.7 %slice-start.1 = ((s8[4718592]{0:T(1024)(128)(4,1)}), s8[524288]{0:T(1024)(128)(4,1)S(1)}, s32[]{:S(2)}) async-start(s8[4718592]{0:T(1024)(128)(4,1)} %bitcast.68), calls=%async_computation.2 | async-start | bytes 1048576
  106.1 56.4 %collective-permute-start.10 = (bf16[3,512,512]{2,1,0:T(8,128)(2,1)}, bf16[3,512,512]{2,1,0:T(8,128)(2,1)}, u32[]{:S(2)}, u32[]{:S(2)}) collective-permute-start(bf16[3,512,512]{2,1,0:T(8,128)(2,1)} %collective-permute-done.9), channel_id=1, source_target_pairs={{0,16},{16,32},{32,48},{48,64},{64,80},{80,96},{96,112},{112,128},... | collective-permute-start | bytes 4718600 | tf_op jit(solution)/shard_map/ppermute | solution.py:11
  159.8 66.3 %collective-permute-start.2 = (bf16[3,512,512]{2,1,0:T(8,128)(2,1)}, bf16[3,512,512]{2,1,0:T(8,128)(2,1)S(1)}, u32[]{:S(2)}, u32[]{:S(2)}) collective-permute-start(bf16[3,512,512]{2,1,0:T(8,128)(2,1)} %collective-permute-done.1), channel_id=1, source_target_pairs={{0,1},{1,2},{2,3},{3,4},{4,5},{5,6},{6,7},{7,8},{8,9},{9,10},{10,1... | collective-permute-start | bytes 4718600 | tf_op jit(solution)/shard_map/ppermute | solution.py:11
  162.5 71.5 %collective-permute-start.11 = (bf16[3,512,512]{2,1,0:T(8,128)(2,1)}, bf16[3,512,512]{2,1,0:T(8,128)(2,1)}, u32[]{:S(2)}, u32[]{:S(2)}) collective-permute-start(bf16[3,512,512]{2,1,0:T(8,128)(2,1)} %collective-permute-done.10), channel_id=1, source_target_pairs={{0,16},{16,32},{32,48},{48,64},{64,80},{80,96},{96,112},{112,128},... | collective-permute-start | bytes 4718600 | tf_op jit(solution)/shard_map/ppermute | solution.py:11
  226.1 8.0 %copy-start.10 = (bf16[3,512,512]{2,1,0:T(8,128)(2,1)}, bf16[3,512,512]{2,1,0:T(8,128)(2,1)S(1)}, u32[]{:S(2)}) copy-start(bf16[3,512,512]{2,1,0:T(8,128)(2,1)S(1)} %collective-permute-done.2) | copy-start | bytes 4718596
  226.1 50.4 %collective-permute-start.3 = (bf16[3,512,512]{2,1,0:T(8,128)(2,1)S(1)}, bf16[3,512,512]{2,1,0:T(8,128)(2,1)}, u32[]{:S(2)}, u32[]{:S(2)}) collective-permute-start(bf16[3,512,512]{2,1,0:T(8,128)(2,1)S(1)} %collective-permute-done.2), channel_id=1, source_target_pairs={{0,1},{1,2},{2,3},{3,4},{4,5},{5,6},{6,7},{7,8},{8,9},{9,10},{10,1... | collective-permute-start | bytes 4718600 | tf_op jit(solution)/shard_map/ppermute | solution.py:11
  234.1 93.5 %collective-permute-start.12 = (bf16[3,512,512]{2,1,0:T(8,128)(2,1)}, bf16[3,512,512]{2,1,0:T(8,128)(2,1)}, u32[]{:S(2)}, u32[]{:S(2)}) collective-permute-start(bf16[3,512,512]{2,1,0:T(8,128)(2,1)} %collective-permute-done.11), channel_id=1, source_target_pairs={{0,128},{16,144},{32,160},{48,176},{64,192},{80,208},{96,224},{112... | collective-permute-start | bytes 4718600 | tf_op jit(solution)/shard_map/ppermute | solution.py:11
  276.5 47.0 %collective-permute-start.4 = (bf16[3,512,512]{2,1,0:T(8,128)(2,1)}, bf16[3,512,512]{2,1,0:T(8,128)(2,1)}, u32[]{:S(2)}, u32[]{:S(2)}) collective-permute-start(bf16[3,512,512]{2,1,0:T(8,128)(2,1)} %collective-permute-done.3), channel_id=1, source_target_pairs={{0,8},{1,9},{2,10},{3,11},{4,12},{5,13},{6,14},{7,15},{8,0},{9,1},... | collective-permute-start | bytes 4718600 | tf_op jit(solution)/shard_map/ppermute | solution.py:11
  299.0 13.1 %copy-start.13 = (s32[3]{0:T(128)S(1)}, s32[3]{0:T(128)}, u32[]{:S(2)}) copy-start(s32[3]{0:T(128)} %param.5) | copy-start | bytes 40
  312.0 11.5 %copy-start.6 = (bf16[512,512,1]{1,0,2:T(8,128)(2,1)S(1)}, bf16[512,512,1]{1,0,2:T(8,128)(2,1)}, u32[]{:S(2)}) copy-start(bf16[512,512,1]{1,0,2:T(8,128)(2,1)} %reshape.26) | copy-start | bytes 1572868
  315.8 11.9 %copy-start.7 = (bf16[512,512,1]{1,0,2:T(8,128)(2,1)S(1)}, bf16[512,512,1]{1,0,2:T(8,128)(2,1)}, u32[]{:S(2)}) copy-start(bf16[512,512,1]{1,0,2:T(8,128)(2,1)} %reshape.27) | copy-start | bytes 1572868
  323.5 101.8 %collective-permute-start.5 = (bf16[3,512,512]{2,1,0:T(8,128)(2,1)}, bf16[3,512,512]{2,1,0:T(8,128)(2,1)}, u32[]{:S(2)}, u32[]{:S(2)}) collective-permute-start(bf16[3,512,512]{2,1,0:T(8,128)(2,1)} %collective-permute-done.4), channel_id=1, source_target_pairs={{0,1},{1,2},{2,3},{3,4},{4,5},{5,6},{6,7},{7,8},{8,9},{9,10},{10,1... | collective-permute-start | bytes 4718600 | tf_op jit(solution)/shard_map/ppermute | solution.py:11
  327.5 100.5 %collective-permute-start.13 = (bf16[3,512,512]{2,1,0:T(8,128)(2,1)}, bf16[3,512,512]{2,1,0:T(8,128)(2,1)}, u32[]{:S(2)}, u32[]{:S(2)}) collective-permute-start(bf16[3,512,512]{2,1,0:T(8,128)(2,1)} %collective-permute-done.12), channel_id=1, source_target_pairs={{0,16},{16,32},{32,48},{48,64},{64,80},{80,96},{96,112},{112,128},... | collective-permute-start | bytes 4718600 | tf_op jit(solution)/shard_map/ppermute | solution.py:11
  414.0 4.3 copy-start
  418.3 4.3 copy-start.9
  425.3 2.8 copy-start.5
  425.3 2.8 copy-start.11
  425.3 57.4 %collective-permute-start.6 = (bf16[3,512,512]{2,1,0:T(8,128)(2,1)}, bf16[3,512,512]{2,1,0:T(8,128)(2,1)S(1)}, u32[]{:S(2)}, u32[]{:S(2)}) collective-permute-start(bf16[3,512,512]{2,1,0:T(8,128)(2,1)} %collective-permute-done.5), channel_id=1, source_target_pairs={{0,1},{1,2},{2,3},{3,4},{4,5},{5,6},{6,7},{7,8},{8,9},{9,10},{10,1... | collective-permute-start | bytes 4718600 | tf_op jit(solution)/shard_map/ppermute | solution.py:11
  428.0 58.7 %collective-permute-start.14 = (bf16[3,512,512]{2,1,0:T(8,128)(2,1)}, bf16[3,512,512]{2,1,0:T(8,128)(2,1)S(1)}, u32[]{:S(2)}, u32[]{:S(2)}) collective-permute-start(bf16[3,512,512]{2,1,0:T(8,128)(2,1)} %collective-permute-done.13), channel_id=1, source_target_pairs={{0,16},{16,32},{32,48},{48,64},{64,80},{80,96},{96,112},{112,128},... | collective-permute-start | bytes 4718600 | tf_op jit(solution)/shard_map/ppermute | solution.py:11
  430.7 4.2 copy-start.4
  438.9 43.7 %copy-start.3 = (bf16[512,512,1]{1,0,2:T(8,128)(2,1)S(1)}, bf16[512,512,1]{1,0,2:T(8,128)(2,1)}, u32[]{:S(2)}) copy-start(bf16[512,512,1]{1,0,2:T(8,128)(2,1)} %reshape.30) | copy-start | bytes 1572868
  482.6 57.2 %collective-permute-start.7 = (bf16[3,512,512]{2,1,0:T(8,128)(2,1)S(1)}, bf16[3,512,512]{2,1,0:T(8,128)(2,1)S(1)}, u32[]{:S(2)}, u32[]{:S(2)}) collective-permute-start(bf16[3,512,512]{2,1,0:T(8,128)(2,1)S(1)} %collective-permute-done.6), channel_id=1, source_target_pairs={{0,1},{1,2},{2,3},{3,4},{4,5},{5,6},{6,7},{7,8},{8,9},{9,10},{10,1... | collective-permute-start | bytes 4718600 | tf_op jit(solution)/shard_map/ppermute | solution.py:11
  486.7 4.4 copy-start.2
  486.7 55.7 %collective-permute-start.15 = (bf16[3,512,512]{2,1,0:T(8,128)(2,1)S(1)}, bf16[3,512,512]{2,1,0:T(8,128)(2,1)}, u32[]{:S(2)}, u32[]{:S(2)}) collective-permute-start(bf16[3,512,512]{2,1,0:T(8,128)(2,1)S(1)} %collective-permute-done.14), channel_id=1, source_target_pairs={{0,16},{16,32},{32,48},{48,64},{64,80},{80,96},{96,112},{112,128},... | collective-permute-start | bytes 4718600 | tf_op jit(solution)/shard_map/ppermute | solution.py:11
  495.2 2.7 copy-start.1
Sparse Core Ops, SparseCore 0:
  162.7 251.2 all-reduce.1
where the time goes:
time: 583 us; the launch traced here: 573 us
  waiting for transfers between devices  419 us (72%)
  matrix products  84.8 us (15%)
  local copies, waits for them, and re-layouts  36.4 us (6%)
  other arithmetic  13.8 us (2%)
  between operations  13.8 us (2%)
    ppermute x16, waiting for transfers between devices, from_behind(): lax.ppermute(array, axis, [(i, (i + by) % length) for i in range(length)])  336 us
    psum x1, waiting for transfers between devices, broadcast(): return lax.psum(jnp.where(mine, array, jnp.zeros_like(array)), axis)  82.2 us
    dot_general x9, matrix products, left_product(): jnp.einsum('kr,dkc->drc', left_op, right_op, preferred_element_type=jnp.f...  52.9 us
    dot_general x9, matrix products, right_product(): jnp.einsum('drc,ck->drk', left_op, right_op, preferred_element_type=jnp.f...  31.9 us
    slice x10, local copies, waits for them, and re-layouts, col_add(): strip_local[(distance + col_span) * col_width:(distance + col_span + 1) *...  23.8 us
  transfers between devices with their start and end apart: 17, of which 9 were waited for; matrix products, arithmetic and copies ran while one was open for 19% of the time, Pallas kernels for 0%

commit v1 on v0

--- a/solution.py
+++ b/solution.py
@@ -13,7 +13,7 @@
 
 def broadcast(array, axis, root):
     mine = lax.axis_index(axis) == root
-    return lax.psum(jnp.where(mine, array, jnp.zeros_like(array)), axis)
+    return jnp.sum(lax.all_gather(jnp.where(mine, array, jnp.zeros_like(array)), axis), axis=0)
 
 
 def mask_blocks(values, occupancy):

time: 583 us -> 862 us (1.48)
  waiting for transfers between devices: 419 us -> 655 us
  other arithmetic: 13.8 us -> 39.3 us
  starting transfers between devices: 5.73 us -> 21.5 us
    ppermute x16, waiting for transfers between devices: 336 us -> 601 us  [from_behind(): lax.ppermute(array, axis, [(i, (i + by) % length) for i in range(length)])]
    psum x1 -> x0, waiting for transfers between devices: 82.2 us -> none  [broadcast(): return lax.psum(jnp.where(mine, array, jnp.zeros_like(array)), axis)]
    all_gather x0 -> x1, waiting for transfers between devices: none -> 54.3 us  [broadcast(): lax.all_gather(jnp.where(mine, array, jnp.zeros_like(array)), axis)]
    reduce_sum x0 -> x1, other arithmetic: none -> 26.8 us  [broadcast(): jnp.sum(lax.all_gather(jnp.where(mine, array, jnp.zeros_like(array)), axi...]
    ppermute x16, starting transfers between devices: 5.73 us -> 21.5 us  [from_behind(): lax.ppermute(array, axis, [(i, (i + by) % length) for i in range(length)])]
  transfers between devices with their start and end apart: 17 -> 17, of which waited for: 9 -> 10; matrix products, arithmetic and copies ran while one was open for 19% -> 14% of each run, Pallas kernels for 0% -> 0%
where the time goes in v1:
time: 862 us; the launch traced here: 851 us
  waiting for transfers between devices  655 us (76%)
  matrix products  79.3 us (9%)
  local copies, waits for them, and re-layouts  41.1 us (5%)
  other arithmetic  39.3 us (5%)
  starting transfers between devices  21.5 us (2%)
  between operations  14 us (2%)
    ppermute x16, waiting for transfers between devices, from_behind(): lax.ppermute(array, axis, [(i, (i + by) % length) for i in range(length)])  601 us
    all_gather x1, waiting for transfers between devices, broadcast(): lax.all_gather(jnp.where(mine, array, jnp.zeros_like(array)), axis)  54.3 us
    dot_general x9, matrix products, left_product(): jnp.einsum('kr,dkc->drc', left_op, right_op, preferred_element_type=jnp.f...  50.9 us
    dot_general x9, matrix products, right_product(): jnp.einsum('drc,ck->drk', left_op, right_op, preferred_element_type=jnp.f...  28.4 us
    reduce_sum x1, other arithmetic, broadcast(): jnp.sum(lax.all_gather(jnp.where(mine, array, jnp.zeros_like(array)), axi...  26.8 us
    slice x10, local copies, waits for them, and re-layouts, col_add(): strip_local[(distance + col_span) * col_width:(distance + col_span + 1) *...  22.6 us
    ppermute x16, starting transfers between devices, from_behind(): lax.ppermute(array, axis, [(i, (i + by) % length) for i in range(length)])  21.5 us
  transfers between devices with their start and end apart: 17, of which 10 were waited for; matrix products, arithmetic and copies ran while one was open for 14% of the time, Pallas kernels for 0%

profile of v1, /device:TPU:2, one launch (start us, length us, event | category | flops | bytes accessed | tf_op | source)
XLA Modules:
  0.0 850.6 jit_solution(3747582813442363438)
XLA Ops:
  6.5 0.8 copy.24
  7.3 0.1 fusion.12
  7.4 0.1 copy.27
  7.5 2.5 mul.60
  10.1 1.0 copy.65
  11.0 1.2 slice-done
  12.2 0.1 slice-done.1
  12.3 2.8 multiply_select_fusion
  15.2 0.9 dynamic-slice_convert_fusion
  16.0 0.3 mul.56
  16.4 0.1 copy.64
  16.5 0.1 copy-done.9
  16.6 0.2 broadcast_multiply_fusion.1
  16.8 0.1 collective-permute-start
  16.8 2.0 collective-permute-start.8
  18.8 78.7 %collective-permute-done = bf16[3,512,512]{2,1,0:T(8,128)(2,1)S(1)} collective-permute-done((bf16[3,512,512]{2,1,0:T(8,128)(2,1)S(1)}, bf16[3,512,512]{2,1,0:T(8,128)(2,1)S(1)}, u32[]{:S(2)}, u32[]{:S(2)}) %collective-permute-start) | collective-permute-done | bytes 1572896 | tf_op jit(solution)/shard_map/ppermute | solution.py:11
  97.6 1.2 copy-done.10
  98.8 76.4 %collective-permute-done.1 = bf16[3,512,512]{2,1,0:T(8,128)(2,1)S(1)} collective-permute-done((bf16[3,512,512]{2,1,0:T(8,128)(2,1)S(1)}, bf16[3,512,512]{2,1,0:T(8,128)(2,1)S(1)}, u32[]{:S(2)}, u32[]{:S(2)}) %collective-permute-start.1) | collective-permute-done | bytes 1572896 | tf_op jit(solution)/shard_map/ppermute | solution.py:11
  175.2 1.2 copy-done.12
  176.4 55.5 %collective-permute-done.2 = bf16[3,512,512]{2,1,0:T(8,128)(2,1)S(1)} collective-permute-done((bf16[3,512,512]{2,1,0:T(8,128)(2,1)S(1)}, bf16[3,512,512]{2,1,0:T(8,128)(2,1)S(1)}, u32[]{:S(2)}, u32[]{:S(2)}) %collective-permute-start.2) | collective-permute-done | bytes 1572896 | tf_op jit(solution)/shard_map/ppermute | solution.py:11
  231.9 1.2 copy-done.14
  233.1 97.6 %collective-permute-done.3 = bf16[3,512,512]{2,1,0:T(8,128)(2,1)S(1)} collective-permute-done((bf16[3,512,512]{2,1,0:T(8,128)(2,1)S(1)}, bf16[3,512,512]{2,1,0:T(8,128)(2,1)S(1)}, u32[]{:S(2)}, u32[]{:S(2)}) %collective-permute-start.3) | collective-permute-done | bytes 1572896 | tf_op jit(solution)/shard_map/ppermute | solution.py:11
  330.7 2.9 collective-permute-start.4
  333.6 2.3 collective-permute-start.12
  335.9 54.8 %collective-permute-done.4 = bf16[3,512,512]{2,1,0:T(8,128)(2,1)} collective-permute-done((bf16[3,512,512]{2,1,0:T(8,128)(2,1)S(1)}, bf16[3,512,512]{2,1,0:T(8,128)(2,1)}, u32[]{:S(2)}, u32[]{:S(2)}) %collective-permute-start.4) | collective-permute-done | bytes 1572896 | tf_op jit(solution)/shard_map/ppermute | solution.py:11
  390.7 14.2 %collective-permute-start.5 = (bf16[3,512,512]{2,1,0:T(8,128)(2,1)}, bf16[3,512,512]{2,1,0:T(8,128)(2,1)}, u32[]{:S(2)}, u32[]{:S(2)}) collective-permute-start(bf16[3,512,512]{2,1,0:T(8,128)(2,1)} %collective-permute-done.4), channel_id=1, source_target_pairs={{0,1},{1,2},{2,3},{3,4},{4,5},{5,6},{6,7},{7,8},{8,9},{9,10},{10,1... | collective-permute-start | bytes 4718600 | tf_op jit(solution)/shard_map/ppermute | solution.py:11
  405.0 7.7 reshape.24
  412.7 47.1 %collective-permute-done.12 = bf16[3,512,512]{2,1,0:T(8,128)(2,1)} collective-permute-done((bf16[3,512,512]{2,1,0:T(8,128)(2,1)S(1)}, bf16[3,512,512]{2,1,0:T(8,128)(2,1)}, u32[]{:S(2)}, u32[]{:S(2)}) %collective-permute-start.12) | collective-permute-done | bytes 1572896 | tf_op jit(solution)/shard_map/ppermute | solution.py:11
  459.8 8.5 %broadcast_multiply_fusion = bf16[18,256,2,256]{3,2,1,0:T(2,128)(2,1)} fusion(bf16[18,256,2,256]{3,2,1,0:T(2,128)(2,1)} %reshape.24, bf16[18,2]{1,0:T(8,128)(2,1)S(1)} %copy.27), kind=kLoop, calls=%fused_computation.5 | loop fusion | flops 2359296 | bytes 9437256 | tf_op jit(solution)/shard_map/mul | solution.py:25
  468.3 66.7 %collective-permute-done.5 = bf16[3,512,512]{2,1,0:T(8,128)(2,1)} collective-permute-done((bf16[3,512,512]{2,1,0:T(8,128)(2,1)}, bf16[3,512,512]{2,1,0:T(8,128)(2,1)}, u32[]{:S(2)}, u32[]{:S(2)}) %collective-permute-start.5) | collective-permute-done | bytes 1572896 | tf_op jit(solution)/shard_map/ppermute | solution.py:11
  535.0 5.9 fusion.13
  540.9 1.4 reshape.34
  542.3 2.2 reshape.33
  544.4 2.2 reshape.32
  546.6 2.2 reshape.31
  548.8 2.2 reshape.30
  551.0 2.2 reshape.29
  553.2 2.2 reshape.28
  555.4 1.1 reshape.27
  556.5 1.1 reshape.26
  557.6 0.3 mul.66
  558.1 0.6 copy-done.8
  558.7 2.6 fusion.14
  561.3 2.7 fusion.15
  564.0 2.7 fusion.16
  566.7 59.5 %collective-permute-done.6 = bf16[3,512,512]{2,1,0:T(8,128)(2,1)} collective-permute-done((bf16[3,512,512]{2,1,0:T(8,128)(2,1)}, bf16[3,512,512]{2,1,0:T(8,128)(2,1)}, u32[]{:S(2)}, u32[]{:S(2)}) %collective-permute-start.6) | collective-permute-done | bytes 1572896 | tf_op jit(solution)/shard_map/ppermute | solution.py:11
  626.2 2.7 fusion.17
  628.9 2.7 fusion.18
  631.5 4.2 fusion.19
  635.7 4.1 fusion.20
  639.8 4.1 fusion.21
  643.9 64.7 %collective-permute-done.7 = bf16[3,512,512]{2,1,0:T(8,128)(2,1)S(1)} collective-permute-done((bf16[3,512,512]{2,1,0:T(8,128)(2,1)}, bf16[3,512,512]{2,1,0:T(8,128)(2,1)S(1)}, u32[]{:S(2)}, u32[]{:S(2)}) %collective-permute-start.7) | collective-permute-done | bytes 1572896 | tf_op jit(solution)/shard_map/ppermute | solution.py:11
  708.6 2.7 fusion.22
  711.3 54.3 %all-gather.3.cloned.1.call-done = bf16[73728,512]{1,0:T(8,128)(2,1)} async-done(((bf16[4608,512]{1,0:T(8,128)(2,1)}), bf16[73728,512]{1,0:T(8,128)(2,1)}) %all-gather.3.cloned.1.call-update) | async-done | bytes 75497488 | tf_op jit(solution)/shard_map/all_gather | solution.py:16
  765.6 26.8 %reduce_sum.12 = bf16[4608,512]{1,0:T(8,128)(2,1)} reduce(bf16[16,4608,512]{2,1,0:T(8,128)(2,1)} %bitcast, bf16[]{:T(256)} %constant.38.clone.1), dimensions={0}, to_apply=%region_0.1 | reduce | flops 35389440 | bytes 80216064 | tf_op jit(solution)/shard_map/reduce_sum | solution.py:16
  792.4 3.9 fusion.9
  796.3 4.1 fusion.2
  800.3 4.1 fusion.3
  804.5 4.3 fusion.4
  808.8 2.7 fusion.5
  811.4 2.7 fusion.6
  814.1 2.7 fusion.7
  816.9 2.7 fusion.8
  819.6 23.7 %fusion.1 = bf16[3,512,512]{2,1,0:T(8,128)(2,1)} fusion(f32[3,512,512]{1,2,0:T(8,128)} %fusion.2, f32[3,512,512]{1,2,0:T(8,128)} %fusion.3, f32[3,512,512]{1,2,0:T(8,128)} %fusion.4, bf16[3,512,512]{2,1,0:T(8,128)(2,1)S(1)} %broadcast_multiply_fusion.1, f32[3,512,512]{1,2,0:T(8,128)} %fusion.5, f32[3,512,512]{1,2,0:T(8,128)} %fusion.6, ...), kind=kOutput, calls=%fused_computation.3 | convolution fusion | flops 823394304 | bytes 59768836 | tf_op jit(solution)/shard_map/kr,dkc->drc/dot_general | solution.py:33
  (74 shorter events, 0.2 us)
Async XLA Ops:
  6.5 759.1 %all-gather.3.cloned.1.call-start = ((), (), s32[]{:S(2)}) async-start(), calls=%async_computation | async-start | bytes 80216064 | tf_op jit(solution)/shard_map/all_gather | solution.py:16
  10.0 2.2 slice-start
  10.1 2.3 slice-start.1
  15.1 1.4 copy-start.9
  16.8 80.8 %collective-permute-start = (bf16[3,512,512]{2,1,0:T(8,128)(2,1)S(1)}, bf16[3,512,512]{2,1,0:T(8,128)(2,1)S(1)}, u32[]{:S(2)}, u32[]{:S(2)}) collective-permute-start(bf16[3,512,512]{2,1,0:T(8,128)(2,1)S(1)} %broadcast_multiply_fusion.1), channel_id=1, source_target_pairs={{0,1},{1,2},{2,3},{3,4},{4,5},{5,6},{6,7},{7,8},{8,9},{9,10},{10,1... | collective-permute-start | bytes 4718600 | tf_op jit(solution)/shard_map/ppermute | solution.py:11
  16.8 80.7 %collective-permute-start.8 = (bf16[3,512,512]{2,1,0:T(8,128)(2,1)S(1)}, bf16[3,512,512]{2,1,0:T(8,128)(2,1)S(1)}, u32[]{:S(2)}, u32[]{:S(2)}) collective-permute-start(bf16[3,512,512]{2,1,0:T(8,128)(2,1)S(1)} %broadcast_multiply_fusion.1), channel_id=1, source_target_pairs={{0,16},{16,32},{32,48},{48,64},{64,80},{80,96},{96,112},{112,128},... | collective-permute-start | bytes 4718600 | tf_op jit(solution)/shard_map/ppermute | solution.py:11
  97.6 236.0 %copy-start.18 = (bf16[3,512,512]{2,1,0:T(8,128)(2,1)}, bf16[3,512,512]{2,1,0:T(8,128)(2,1)S(1)}, u32[]{:S(2)}) copy-start(bf16[3,512,512]{2,1,0:T(8,128)(2,1)S(1)} %collective-permute-done) | copy-start | bytes 4718596
  97.6 77.6 %collective-permute-start.1 = (bf16[3,512,512]{2,1,0:T(8,128)(2,1)S(1)}, bf16[3,512,512]{2,1,0:T(8,128)(2,1)S(1)}, u32[]{:S(2)}, u32[]{:S(2)}) collective-permute-start(bf16[3,512,512]{2,1,0:T(8,128)(2,1)S(1)} %collective-permute-done), channel_id=1, source_target_pairs={{0,1},{1,2},{2,3},{3,4},{4,5},{5,6},{6,7},{7,8},{8,9},{9,10},{10,1... | collective-permute-start | bytes 4718600 | tf_op jit(solution)/shard_map/ppermute | solution.py:11
  97.6 1.2 copy-start.10
  98.8 76.4 %collective-permute-start.9 = (bf16[3,512,512]{2,1,0:T(8,128)(2,1)S(1)}, bf16[3,512,512]{2,1,0:T(8,128)(2,1)S(1)}, u32[]{:S(2)}, u32[]{:S(2)}) collective-permute-start(bf16[3,512,512]{2,1,0:T(8,128)(2,1)S(1)} %collective-permute-done.8), channel_id=1, source_target_pairs={{0,16},{16,32},{32,48},{48,64},{64,80},{80,96},{96,112},{112,128},... | collective-permute-start | bytes 4718600 | tf_op jit(solution)/shard_map/ppermute | solution.py:11
  175.2 160.7 %copy-start.20 = (bf16[3,512,512]{2,1,0:T(8,128)(2,1)}, bf16[3,512,512]{2,1,0:T(8,128)(2,1)S(1)}, u32[]{:S(2)}) copy-start(bf16[3,512,512]{2,1,0:T(8,128)(2,1)S(1)} %collective-permute-done.1) | copy-start | bytes 4718596
  175.2 56.7 %collective-permute-start.2 = (bf16[3,512,512]{2,1,0:T(8,128)(2,1)S(1)}, bf16[3,512,512]{2,1,0:T(8,128)(2,1)S(1)}, u32[]{:S(2)}, u32[]{:S(2)}) collective-permute-start(bf16[3,512,512]{2,1,0:T(8,128)(2,1)S(1)} %collective-permute-done.1), channel_id=1, source_target_pairs={{0,1},{1,2},{2,3},{3,4},{4,5},{5,6},{6,7},{7,8},{8,9},{9,10},{10,1... | collective-permute-start | bytes 4718600 | tf_op jit(solution)/shard_map/ppermute | solution.py:11
  175.2 1.2 copy-start.12
  176.4 55.5 %collective-permute-start.10 = (bf16[3,512,512]{2,1,0:T(8,128)(2,1)S(1)}, bf16[3,512,512]{2,1,0:T(8,128)(2,1)S(1)}, u32[]{:S(2)}, u32[]{:S(2)}) collective-permute-start(bf16[3,512,512]{2,1,0:T(8,128)(2,1)S(1)} %collective-permute-done.9), channel_id=1, source_target_pairs={{0,16},{16,32},{32,48},{48,64},{64,80},{80,96},{96,112},{112,128},... | collective-permute-start | bytes 4718600 | tf_op jit(solution)/shard_map/ppermute | solution.py:11
  231.9 158.8 %copy-start.22 = (bf16[3,512,512]{2,1,0:T(8,128)(2,1)}, bf16[3,512,512]{2,1,0:T(8,128)(2,1)S(1)}, u32[]{:S(2)}) copy-start(bf16[3,512,512]{2,1,0:T(8,128)(2,1)S(1)} %collective-permute-done.2) | copy-start | bytes 4718596
  231.9 98.8 %collective-permute-start.3 = (bf16[3,512,512]{2,1,0:T(8,128)(2,1)S(1)}, bf16[3,512,512]{2,1,0:T(8,128)(2,1)S(1)}, u32[]{:S(2)}, u32[]{:S(2)}) collective-permute-start(bf16[3,512,512]{2,1,0:T(8,128)(2,1)S(1)} %collective-permute-done.2), channel_id=1, source_target_pairs={{0,1},{1,2},{2,3},{3,4},{4,5},{5,6},{6,7},{7,8},{8,9},{9,10},{10,1... | collective-permute-start | bytes 4718600 | tf_op jit(solution)/shard_map/ppermute | solution.py:11
  231.9 1.2 copy-start.14
  233.1 100.5 %collective-permute-start.11 = (bf16[3,512,512]{2,1,0:T(8,128)(2,1)S(1)}, bf16[3,512,512]{2,1,0:T(8,128)(2,1)S(1)}, u32[]{:S(2)}, u32[]{:S(2)}) collective-permute-start(bf16[3,512,512]{2,1,0:T(8,128)(2,1)S(1)} %collective-permute-done.10), channel_id=1, source_target_pairs={{0,16},{16,32},{32,48},{48,64},{64,80},{80,96},{96,112},{112,128},... | collective-permute-start | bytes 4718600 | tf_op jit(solution)/shard_map/ppermute | solution.py:11
  330.7 60.0 %copy-start.24 = (bf16[3,512,512]{2,1,0:T(8,128)(2,1)}, bf16[3,512,512]{2,1,0:T(8,128)(2,1)S(1)}, u32[]{:S(2)}) copy-start(bf16[3,512,512]{2,1,0:T(8,128)(2,1)S(1)} %collective-permute-done.3) | copy-start | bytes 4718596
  330.7 60.0 %collective-permute-start.4 = (bf16[3,512,512]{2,1,0:T(8,128)(2,1)S(1)}, bf16[3,512,512]{2,1,0:T(8,128)(2,1)}, u32[]{:S(2)}, u32[]{:S(2)}) collective-permute-start(bf16[3,512,512]{2,1,0:T(8,128)(2,1)S(1)} %collective-permute-done.3), channel_id=1, source_target_pairs={{0,8},{1,9},{2,10},{3,11},{4,12},{5,13},{6,14},{7,15},{8,0},{9,1},... | collective-permute-start | bytes 4718600 | tf_op jit(solution)/shard_map/ppermute | solution.py:11
  333.6 79.1 %copy-start.16 = (bf16[3,512,512]{2,1,0:T(8,128)(2,1)}, bf16[3,512,512]{2,1,0:T(8,128)(2,1)S(1)}, u32[]{:S(2)}) copy-start(bf16[3,512,512]{2,1,0:T(8,128)(2,1)S(1)} %collective-permute-done.11) | copy-start | bytes 4718596
  333.6 126.2 %collective-permute-start.12 = (bf16[3,512,512]{2,1,0:T(8,128)(2,1)S(1)}, bf16[3,512,512]{2,1,0:T(8,128)(2,1)}, u32[]{:S(2)}, u32[]{:S(2)}) collective-permute-start(bf16[3,512,512]{2,1,0:T(8,128)(2,1)S(1)} %collective-permute-done.11), channel_id=1, source_target_pairs={{0,128},{16,144},{32,160},{48,176},{64,192},{80,208},{96,224},{112... | collective-permute-start | bytes 4718600 | tf_op jit(solution)/shard_map/ppermute | solution.py:11
  390.7 144.3 %collective-permute-start.5 = (bf16[3,512,512]{2,1,0:T(8,128)(2,1)}, bf16[3,512,512]{2,1,0:T(8,128)(2,1)}, u32[]{:S(2)}, u32[]{:S(2)}) collective-permute-start(bf16[3,512,512]{2,1,0:T(8,128)(2,1)} %collective-permute-done.4), channel_id=1, source_target_pairs={{0,1},{1,2},{2,3},{3,4},{4,5},{5,6},{6,7},{7,8},{8,9},{9,10},{10,1... | collective-permute-start | bytes 4718600 | tf_op jit(solution)/shard_map/ppermute | solution.py:11
  459.8 104.2 %collective-permute-start.13 = (bf16[3,512,512]{2,1,0:T(8,128)(2,1)}, bf16[3,512,512]{2,1,0:T(8,128)(2,1)}, u32[]{:S(2)}, u32[]{:S(2)}) collective-permute-start(bf16[3,512,512]{2,1,0:T(8,128)(2,1)} %collective-permute-done.12), channel_id=1, source_target_pairs={{0,16},{16,32},{32,48},{48,64},{64,80},{80,96},{96,112},{112,128},... | collective-permute-start | bytes 4718600 | tf_op jit(solution)/shard_map/ppermute | solution.py:11
  535.0 91.2 %collective-permute-start.6 = (bf16[3,512,512]{2,1,0:T(8,128)(2,1)}, bf16[3,512,512]{2,1,0:T(8,128)(2,1)}, u32[]{:S(2)}, u32[]{:S(2)}) collective-permute-start(bf16[3,512,512]{2,1,0:T(8,128)(2,1)} %collective-permute-done.5), channel_id=1, source_target_pairs={{0,1},{1,2},{2,3},{3,4},{4,5},{5,6},{6,7},{7,8},{8,9},{9,10},{10,1... | collective-permute-start | bytes 4718600 | tf_op jit(solution)/shard_map/ppermute | solution.py:11
  553.2 4.9 copy-start.26
  557.6 1.0 copy-start.8
  558.1 3.2 copy-start.7
  558.1 3.2 copy-start.19
  561.3 2.7 copy-start.6
  561.3 2.7 copy-start.21
  564.0 62.2 %copy-start.5 = (bf16[512,512,1]{1,0,2:T(8,128)(2,1)S(1)}, bf16[512,512,1]{1,0,2:T(8,128)(2,1)}, u32[]{:S(2)}) copy-start(bf16[512,512,1]{1,0,2:T(8,128)(2,1)} %reshape.29) | copy-start | bytes 1572868
  564.0 62.2 %copy-start.23 = (bf16[3,512,512]{2,1,0:T(8,128)(2,1)S(1)}, bf16[3,512,512]{2,1,0:T(8,128)(2,1)}, u32[]{:S(2)}) copy-start(bf16[3,512,512]{2,1,0:T(8,128)(2,1)} %copy-done.22) | copy-start | bytes 4718596
  564.0 75.8 %collective-permute-start.14 = (bf16[3,512,512]{2,1,0:T(8,128)(2,1)}, bf16[3,512,512]{2,1,0:T(8,128)(2,1)}, u32[]{:S(2)}, u32[]{:S(2)}) collective-permute-start(bf16[3,512,512]{2,1,0:T(8,128)(2,1)} %collective-permute-done.13), channel_id=1, source_target_pairs={{0,16},{16,32},{32,48},{48,64},{64,80},{80,96},{96,112},{112,128},... | collective-permute-start | bytes 4718600 | tf_op jit(solution)/shard_map/ppermute | solution.py:11
  566.7 62.2 %copy-start.4 = (bf16[512,512,1]{1,0,2:T(8,128)(2,1)S(1)}, bf16[512,512,1]{1,0,2:T(8,128)(2,1)}, u32[]{:S(2)}) copy-start(bf16[512,512,1]{1,0,2:T(8,128)(2,1)} %reshape.30) | copy-start | bytes 1572868
  566.7 62.2 %copy-start.25 = (bf16[3,512,512]{2,1,0:T(8,128)(2,1)S(1)}, bf16[3,512,512]{2,1,0:T(8,128)(2,1)}, u32[]{:S(2)}) copy-start(bf16[3,512,512]{2,1,0:T(8,128)(2,1)} %copy-done.24) | copy-start | bytes 4718596
  626.2 82.4 %collective-permute-start.7 = (bf16[3,512,512]{2,1,0:T(8,128)(2,1)}, bf16[3,512,512]{2,1,0:T(8,128)(2,1)S(1)}, u32[]{:S(2)}, u32[]{:S(2)}) collective-permute-start(bf16[3,512,512]{2,1,0:T(8,128)(2,1)} %collective-permute-done.6), channel_id=1, source_target_pairs={{0,1},{1,2},{2,3},{3,4},{4,5},{5,6},{6,7},{7,8},{8,9},{9,10},{10,1... | collective-permute-start | bytes 4718600 | tf_op jit(solution)/shard_map/ppermute | solution.py:11
  628.9 2.7 copy-start.3
  631.5 4.2 copy-start.2
  635.7 4.1 copy-start.1
  639.8 179.8 %collective-permute-start.15 = (bf16[3,512,512]{2,1,0:T(8,128)(2,1)}, bf16[3,512,512]{2,1,0:T(8,128)(2,1)}, u32[]{:S(2)}, u32[]{:S(2)}) collective-permute-start(bf16[3,512,512]{2,1,0:T(8,128)(2,1)} %collective-permute-done.14), channel_id=1, source_target_pairs={{0,16},{16,32},{32,48},{48,64},{64,80},{80,96},{96,112},{112,128},... | collective-permute-start | bytes 4718600 | tf_op jit(solution)/shard_map/ppermute | solution.py:11
  792.4 3.9 copy-start
  804.5 4.3 copy-start.17
  808.8 2.7 copy-start.15
  811.4 2.7 copy-start.13
  814.1 2.8 copy-start.11
Sparse Core Ops, SparseCore 0:
  15.3 750.2 all-gather.2
